TPU v7x, 128 devices: a whole 4x4x4 slice. The times are simulated.
128 devices in a mesh: dp: 32 (over x, z_hi, y), tensor: 4 (over z_lo, core).
Axes of the slice: x: 4, y: 4, z: 4 (z_hi: 2, z_lo: 2; z = z_hi * 2 + z_lo), core: 2. Of those that a mesh axis runs over, the one named last changes fastest.
Arguments:
- tokens: bfloat16 [65536, 1024], P(('dp', 'tensor')), may hold values from -16 to 16
- prompts: bfloat16 [32, 64, 1024], P('dp'), may hold values from -6 to 6
- w_attn: bfloat16 [3, 1024, 1024], P(None, None, 'tensor'), may hold values from -0.1875 to 0.1875
- w_out: bfloat16 [1024, 1024], P('tensor'), may hold values from -0.1875 to 0.1875
- norm_gain: float32 [2, 1024], replicated, may hold values from 0.1 to 1.9
- norm_bias: float32 [2, 1024], replicated, may hold values from -3 to 3
- w_in: bfloat16 [1024, 4096], P(None, 'tensor'), may hold values from -0.1875 to 0.1875
- b_in: float32 [4096], P('tensor'), may hold values from -3 to 3
- w_down: bfloat16 [4096, 1024], P('tensor'), may hold values from -0.09375 to 0.09375
- index_rows: bfloat16 [65536, 1024], P('dp'), may hold values from -6 to 6
- lengths: int32 [32, 32], P('dp'), may hold values from 1 to 512, 2048 in all within a row
- groups: int32 [1024], P('dp'), may hold values from 0 to 31
- candidates: int32 [1024, 64], P(('dp', 'tensor')), may hold values from 0 to 65535
Outputs:
- scores: float32 [1024, 64], P(('dp', 'tensor'))
All inputs are finite; a program needn't handle non-finite values.
Results may differ from a plain program's by a relative error of at most 0.01.
Values may be sent and summed in bfloat16 or wider, within the bound.
No kernel may reach another device: no remote copies, remote signals or barrier semaphores. Data moves between devices by JAX's collectives and lax.ppermute only.
A program may use at most 128 MiB of HBM per device.

v0:
```python
import jax
import jax.numpy as jnp
from jax import lax
from jax.sharding import PartitionSpec as P

D = 1024
HEAD_DIM = 64


def layer_norm(values, gain, bias):
    mean = jnp.mean(values, axis=-1, keepdims=True)
    centred = values - mean
    var = jnp.mean(centred * centred, axis=-1, keepdims=True)
    return centred * lax.rsqrt(var + 1e-05) * gain + bias


def project(block, weight):
    return jnp.dot(block, weight, preferred_element_type=jnp.float32).astype(jnp.bfloat16)


def shards(
    tokens,
    prompts,
    w_attn,
    w_out,
    norm_gain,
    norm_bias,
    w_in,
    b_in,
    w_down,
    index_rows,
    lengths,
    groups,
    candidates,
):
    shard_rows = tokens.shape[0]
    tok_dev = shard_rows * lax.axis_size("tensor")
    columns = w_attn.shape[2]
    heads_here = columns // HEAD_DIM
    scale = HEAD_DIM ** (-0.5)
    whole = lax.all_gather(tokens, "tensor", axis=0, tiled=True)
    query = (jnp.dot(whole, w_attn[0], preferred_element_type=jnp.float32) * scale).astype(
        jnp.bfloat16
    )
    keys = project(whole, w_attn[1])
    values = project(whole, w_attn[2])
    every_prompt = lax.all_gather(prompts, "dp", axis=0, tiled=True)
    flat = every_prompt.reshape(-1, every_prompt.shape[2])
    prompt_key = project(flat, w_attn[1])
    prompt_value = project(flat, w_attn[2])
    prompt_len = prompts.shape[1]
    prompt_rows = prompt_key.shape[0]
    lens = lengths[0]
    texts_here = lens.shape[0]
    text_ids = jnp.arange(texts_here, dtype=jnp.int32)
    ends = jnp.cumsum(lens)
    position = jnp.arange(tok_dev, dtype=jnp.int32)
    seg = jnp.sum((position[:, None] >= ends[None, :]).astype(jnp.int32), axis=1)
    tok_group = jnp.sum(jnp.where(seg[:, None] == text_ids[None, :], groups[None, :], 0), axis=1)
    key_group = jnp.arange(prompt_rows, dtype=jnp.int32) // prompt_len
    all_keys = jnp.concatenate([keys, prompt_key], axis=0).reshape(-1, heads_here, HEAD_DIM)
    all_values = jnp.concatenate([values, prompt_value], axis=0).reshape(-1, heads_here, HEAD_DIM)
    block = min(512, tok_dev)

    def attend(number):
        start = number * block
        q_block = lax.dynamic_slice_in_dim(query, start, block, 0).reshape(
            block, heads_here, HEAD_DIM
        )
        seg_block = lax.dynamic_slice_in_dim(seg, start, block, 0)
        group_block = lax.dynamic_slice_in_dim(tok_group, start, block, 0)
        allowed = jnp.concatenate(
            [seg_block[:, None] == seg[None, :], group_block[:, None] == key_group[None, :]], axis=1
        )
        logits = jnp.einsum("qhe,khe->hqk", q_block, all_keys, preferred_element_type=jnp.float32)
        logits = jnp.where(allowed[None], logits, jnp.float32(-1e30))
        top = jnp.max(logits, axis=2, keepdims=True)
        weights = jnp.exp(logits - top)
        total = jnp.sum(weights, axis=2, keepdims=True)
        probs = (weights / total).astype(jnp.bfloat16)
        mixed = jnp.einsum("hqk,khe->qhe", probs, all_values, preferred_element_type=jnp.float32)
        return mixed.astype(jnp.bfloat16).reshape(block, columns)

    context = lax.map(attend, jnp.arange(tok_dev // block, dtype=jnp.int32)).reshape(
        tok_dev, columns
    )
    my_start = lax.axis_index("tensor") * shard_rows
    attn_part = lax.psum_scatter(
        jnp.dot(context, w_out, preferred_element_type=jnp.float32),
        "tensor",
        scatter_dimension=0,
        tiled=True,
    )
    normed_rows = layer_norm(
        tokens.astype(jnp.float32) + attn_part, norm_gain[0], norm_bias[0]
    ).astype(jnp.bfloat16)
    expanded = jax.nn.gelu(
        jnp.dot(
            lax.all_gather(normed_rows, "tensor", axis=0, tiled=True),
            w_in,
            preferred_element_type=jnp.float32,
        )
        + b_in,
        approximate=False,
    ).astype(jnp.bfloat16)
    reduced = lax.psum_scatter(
        jnp.dot(expanded, w_down, preferred_element_type=jnp.float32).astype(jnp.bfloat16),
        "tensor",
        scatter_dimension=0,
        tiled=True,
    ).astype(jnp.float32)
    output = layer_norm(
        normed_rows.astype(jnp.float32) + reduced, norm_gain[1], norm_bias[1]
    ).astype(jnp.bfloat16)
    seg_rows = lax.dynamic_slice_in_dim(seg, my_start, shard_rows, 0)
    member = (text_ids[:, None] == seg_rows[None, :]).astype(jnp.bfloat16)
    partial_sums = jnp.dot(member, output, preferred_element_type=jnp.float32)
    pooled_sums = lax.psum_scatter(partial_sums, "tensor", scatter_dimension=0, tiled=True)
    mine = pooled_sums.shape[0]
    my_lens = lax.dynamic_slice_in_dim(lens, lax.axis_index("tensor") * mine, mine, 0)
    pooled = pooled_sums / my_lens[:, None].astype(jnp.float32)
    square = jnp.mean(pooled * pooled, axis=1, keepdims=True)
    embedding = (pooled * lax.rsqrt(square + 1e-06)).astype(jnp.bfloat16)
    asked_vectors, asked_rows = (
        lax.all_gather(embedding, "dp", axis=0, tiled=True),
        lax.all_gather(candidates, "dp", axis=0, tiled=True),
    )
    held = index_rows.shape[0]
    local_rows = asked_rows - lax.axis_index("dp") * held
    owned = (local_rows >= 0) & (local_rows < held)
    table = jnp.dot(asked_vectors, index_rows.T, preferred_element_type=jnp.float32) * D ** (-0.5)
    picked = jnp.take_along_axis(table, jnp.clip(local_rows, 0, held - 1), axis=1)
    picked = jnp.where(owned, picked, jnp.float32(0.0))
    return lax.psum_scatter(
        picked.astype(jnp.bfloat16), "dp", scatter_dimension=0, tiled=True
    ).astype(jnp.float32)


def solution(mesh):
    placed = (
        P(("dp", "tensor"), None),
        P("dp", None, None),
        P(None, None, "tensor"),
        P("tensor", None),
        P(),
        P(),
        P(None, "tensor"),
        P("tensor"),
        P("tensor", None),
        P("dp", None),
        P("dp", None),
        P("dp"),
        P(("dp", "tensor"), None),
    )
    return jax.shard_map(
        shards, mesh=mesh, in_specs=placed, out_specs=P(("dp", "tensor"), None), check_vma=False
    )
```

profile of v0, /device:TPU:0, one launch (start us, length us, event | category | flops | bytes accessed | tf_op | source)
XLA Modules:
  0.0 1021.1 jit_solution(8762261364968548644)
XLA Ops:
  9.9 47.5 %all-gather.4.cloned.1.call-done = bf16[2048,1024]{1,0:T(8,128)(2,1)} async-done(((bf16[512,1024]{1,0:T(8,128)(2,1)}), bf16[2048,1024]{1,0:T(8,128)(2,1)}) %all-gather.4.cloned.1.call-update) | async-done | bytes 4194320 | tf_op jit(solution)/shard_map/all_gather | solution.py:41
  57.4 3.7 convolution_convert_fusion.1
  61.5 2.3 convolution_convert_fusion.3
  63.7 2.3 fusion.48
  66.1 78.2 %all-gather.6.cloned.1.call-done = bf16[32,64,1024]{2,1,0:T(8,128)(2,1)} async-done(((bf16[1,64,1024]{2,1,0:T(8,128)(2,1)}), bf16[32,64,1024]{2,1,0:T(8,128)(2,1)}) %all-gather.6.cloned.1.call-update) | async-done | bytes 4194320 | tf_op jit(solution)/shard_map/all_gather | solution.py:47
  144.3 4.7 convolution_convert_fusion
  149.0 2.4 convolution_convert_fusion.2
  152.9 4.1 copy.29
  157.0 2.7 pad_maximum_fusion.1
  159.7 4.1 copy.30
  163.8 158.4 %while.11 = (s32[]{:T(128)}, bf16[4,512,256]{2,1,0:T(8,128)(2,1)}, s32[4]{0:T(128)S(1)}, s32[2048]{0:T(1024)S(1)}, s32[2048]{0:T(1024)S(1)}, /*index=5*/bf16[204...) while((s32[]{:T(128)}, bf16[4,512,256]{2,1,0:T(8,128)(2,1)}, ...), condition=%wide.region_6.7_spmd.clone, body=%wide.region_3.6_spmd.clone.sunk | while | flops 3284297728 | bytes 19714248 | solution.py:84
  169.6 14.5 %fusion.133 = f32[4,512]{1,0:T(4,128)S(1)} fusion(pred[512,4096]{1,0:T(8,128)(4,1)} %pad_add_fusion.2, bf16[512,4,64]{0,2,1:T(8,128)(2,1)S(1)} %bitcast.71, bf16[4096,4,64]{0,2,1:T(8,128)(2,1)} %get-tuple-element.208), kind=kOutput, calls=%fused_computation.127.clone.1 | convolution fusion | flops 1098911744 | bytes 4464640 | tf_op jit(solution)/shard_map/while/body/eval_jaxpr/sub | solution.py:78
  184.0 16.2 %fusion.134 = bf16[4,512,64]{1,2,0:T(8,128)(2,1)S(1)} fusion(bf16[4096,4,64]{0,2,1:T(8,128)(2,1)} %get-tuple-element.209, f32[4,512]{1,0:T(4,128)S(1)} %fusion.133, pred[512,4096]{1,0:T(8,128)(4,1)} %pad_add_fusion.2, bf16[512,4,64]{0,2,1:T(8,128)(2,1)S(1)} %bitcast.72, bf16[4096,4,64]{0,2,1:T(8,128)(2,1)} %get-tuple-element.208), kind=kOutput, calls=%fused_computation.14.clone.1 | convolution fusion | flops 2181175296 | bytes 6823936 | tf_op jit(solution)/shard_map/while/body/eval_jaxpr/hqk,khe->qhe/dot_general | solution.py:81
  206.5 14.5 %fusion.133 = f32[4,512]{1,0:T(4,128)S(1)} fusion(pred[512,4096]{1,0:T(8,128)(4,1)} %pad_add_fusion.2, bf16[512,4,64]{0,2,1:T(8,128)(2,1)S(1)} %bitcast.71, bf16[4096,4,64]{0,2,1:T(8,128)(2,1)} %get-tuple-element.208), kind=kOutput, calls=%fused_computation.127.clone.1 | convolution fusion | flops 1098911744 | bytes 4464640 | tf_op jit(solution)/shard_map/while/body/eval_jaxpr/sub | solution.py:78
  221.0 16.2 %fusion.134 = bf16[4,512,64]{1,2,0:T(8,128)(2,1)S(1)} fusion(bf16[4096,4,64]{0,2,1:T(8,128)(2,1)} %get-tuple-element.209, f32[4,512]{1,0:T(4,128)S(1)} %fusion.133, pred[512,4096]{1,0:T(8,128)(4,1)} %pad_add_fusion.2, bf16[512,4,64]{0,2,1:T(8,128)(2,1)S(1)} %bitcast.72, bf16[4096,4,64]{0,2,1:T(8,128)(2,1)} %get-tuple-element.208), kind=kOutput, calls=%fused_computation.14.clone.1 | convolution fusion | flops 2181175296 | bytes 6823936 | tf_op jit(solution)/shard_map/while/body/eval_jaxpr/hqk,khe->qhe/dot_general | solution.py:81
  243.5 14.5 %fusion.133 = f32[4,512]{1,0:T(4,128)S(1)} fusion(pred[512,4096]{1,0:T(8,128)(4,1)} %pad_add_fusion.2, bf16[512,4,64]{0,2,1:T(8,128)(2,1)S(1)} %bitcast.71, bf16[4096,4,64]{0,2,1:T(8,128)(2,1)} %get-tuple-element.208), kind=kOutput, calls=%fused_computation.127.clone.1 | convolution fusion | flops 1098911744 | bytes 4464640 | tf_op jit(solution)/shard_map/while/body/eval_jaxpr/sub | solution.py:78
  258.0 16.2 %fusion.134 = bf16[4,512,64]{1,2,0:T(8,128)(2,1)S(1)} fusion(bf16[4096,4,64]{0,2,1:T(8,128)(2,1)} %get-tuple-element.209, f32[4,512]{1,0:T(4,128)S(1)} %fusion.133, pred[512,4096]{1,0:T(8,128)(4,1)} %pad_add_fusion.2, bf16[512,4,64]{0,2,1:T(8,128)(2,1)S(1)} %bitcast.72, bf16[4096,4,64]{0,2,1:T(8,128)(2,1)} %get-tuple-element.208), kind=kOutput, calls=%fused_computation.14.clone.1 | convolution fusion | flops 2181175296 | bytes 6823936 | tf_op jit(solution)/shard_map/while/body/eval_jaxpr/hqk,khe->qhe/dot_general | solution.py:81
  280.5 14.5 %fusion.133 = f32[4,512]{1,0:T(4,128)S(1)} fusion(pred[512,4096]{1,0:T(8,128)(4,1)} %pad_add_fusion.2, bf16[512,4,64]{0,2,1:T(8,128)(2,1)S(1)} %bitcast.71, bf16[4096,4,64]{0,2,1:T(8,128)(2,1)} %get-tuple-element.208), kind=kOutput, calls=%fused_computation.127.clone.1 | convolution fusion | flops 1098911744 | bytes 4464640 | tf_op jit(solution)/shard_map/while/body/eval_jaxpr/sub | solution.py:78
  295.0 16.2 %fusion.134 = bf16[4,512,64]{1,2,0:T(8,128)(2,1)S(1)} fusion(bf16[4096,4,64]{0,2,1:T(8,128)(2,1)} %get-tuple-element.209, f32[4,512]{1,0:T(4,128)S(1)} %fusion.133, pred[512,4096]{1,0:T(8,128)(4,1)} %pad_add_fusion.2, bf16[512,4,64]{0,2,1:T(8,128)(2,1)S(1)} %bitcast.72, bf16[4096,4,64]{0,2,1:T(8,128)(2,1)} %get-tuple-element.208), kind=kOutput, calls=%fused_computation.14.clone.1 | convolution fusion | flops 2181175296 | bytes 6823936 | tf_op jit(solution)/shard_map/while/body/eval_jaxpr/hqk,khe->qhe/dot_general | solution.py:81
  322.1 5.8 fusion.97
  328.7 75.2 %reduce-scatter.4.cloned.1.call-done = f32[512,1024]{1,0:T(8,128)} async-done(((f32[2048,1024]{1,0:T(8,128)}), f32[512,1024]{1,0:T(8,128)}) %reduce-scatter.4.cloned.1.call-update) | async-done | bytes 2097168 | tf_op jit(solution)/shard_map/reduce_scatter | solution.py:88
  403.9 2.0 fusion.52
  408.3 46.9 %all-gather.8.cloned.1.call-done = bf16[2048,1024]{1,0:T(8,128)(2,1)} async-done(((bf16[512,1024]{1,0:T(8,128)(2,1)}), bf16[2048,1024]{1,0:T(8,128)(2,1)}) %all-gather.8.cloned.1.call-update) | async-done | bytes 4194320 | tf_op jit(solution)/shard_map/all_gather | solution.py:99
  455.3 28.5 %fusion.43 = bf16[2048,1024]{1,0:T(8,128)(2,1)} fusion(bf16[1024,1024]{1,0:T(8,128)(2,1)S(1)} %copy-done, f32[1024]{0:T(1024)S(1)} %copy-done.13, bf16[2048,1024]{1,0:T(8,128)(2,1)} %all-gather.8.cloned.1.call-done, bf16[1024,1024]{1,0:T(8,128)(2,1)} %param.21), kind=kOutput, calls=%fused_computation.47 | convolution fusion | flops 8730443776 | bytes 12587008 | tf_op jit(solution)/shard_map/dot_general | solution.py:107
  484.5 95.9 %all_gather.15 = s32[256,64]{1,0:T(8,128)S(1)} all-gather(s32[8,64]{1,0:T(8,128)S(1)} %copy-done.8), channel_id=1, replica_groups=mesh['dp'=32,'tensor'=4] {'dp'}, dimensions={0}, use_global_device_ids=true | all-gather | bytes 67584 | tf_op jit(solution)/shard_map/all_gather | solution.py:126
  580.4 1.7 fusion.50
  582.1 1.7 multiply_reduce_fusion
  586.7 9.1 reduce-scatter.8.cloned.1.call-done
  597.6 97.2 %all_gather.19 = bf16[256,1024]{1,0:T(8,128)(2,1)S(1)} all-gather(bf16[8,1024]{1,0:T(8,128)(2,1)S(1)} %multiply_convert_fusion), channel_id=1, replica_groups=mesh['dp'=32,'tensor'=4] {'dp'}, dimensions={0}, use_global_device_ids=true | all-gather | bytes 540672 | tf_op jit(solution)/shard_map/all_gather | solution.py:125
  694.8 3.5 convolution_multiply_fusion
  698.2 138.8 %gather_fusion = bf16[16384]{0:T(1024)(128)(2,1)S(1)} fusion(bf16[256,2048]{1,0:T(8,128)(2,1)S(1)} %convolution_multiply_fusion, s32[16384]{0:T(1024)S(1)} %reshape.112), kind=kCustom, calls=%fused_computation | custom fusion | bytes 196608 | tf_op jit(solution)/shard_map/jit(take_along_axis)/gather | solution.py:132
  837.3 176.2 %all-reduce = bf16[256,64]{1,0:T(8,128)(2,1)S(1)} all-reduce(bf16[256,64]{1,0:T(8,128)(2,1)S(1)} %select_convert_fusion), channel_id=5, replica_groups=mesh['dp'=32,'tensor'=4] {'dp'}, use_global_device_ids=true, to_apply=%region_15.16.clone | all-reduce | flops 16384 | bytes 65536
  (111 shorter events, 35.8 us)
Async XLA Ops:
  6.5 448.7 %copy-start = (bf16[1024,1024]{1,0:T(8,128)(2,1)S(1)}, bf16[1024,1024]{1,0:T(8,128)(2,1)}, u32[]{:S(2)}) copy-start(bf16[1024,1024]{1,0:T(8,128)(2,1)} %param.23) | copy-start | bytes 6291460
  6.5 50.9 %all-gather.4.cloned.1.call-start = ((), (), s32[]{:S(2)}) async-start(), calls=%async_computation.3 | async-start | bytes 5242880 | tf_op jit(solution)/shard_map/all_gather | solution.py:41
  7.3 137.0 %all-gather.6.cloned.1.call-start = ((), (), s32[]{:S(2)}) async-start(), calls=%async_computation.4 | async-start | bytes 4325376 | tf_op jit(solution)/shard_map/all_gather | solution.py:47
  8.0 395.9 %reduce-scatter.4.cloned.1.call-start = ((), (), s32[]{:S(2)}) async-start(), calls=%async_computation.5 | async-start | bytes 10485760 | tf_op jit(solution)/shard_map/reduce_scatter | solution.py:88
  57.4 3.7 copy-start.10
  57.4 4.1 copy-start.12
  144.3 4.7 copy-start.11
  149.0 2.4 copy-start.5
  328.0 0.7 copy-start.6
  328.0 0.7 copy-start.7
  328.0 75.9 %copy-start.3 = (bf16[512,1024]{1,0:T(8,128)(2,1)S(1)}, bf16[512,1024]{1,0:T(8,128)(2,1)}, u32[]{:S(2)}) copy-start(bf16[512,1024]{1,0:T(8,128)(2,1)} %param.15) | copy-start | bytes 3145732
  328.0 127.2 %all-gather.8.cloned.1.call-start = ((), (), s32[]{:S(2)}) async-start(), calls=%async_computation.6 | async-start | bytes 5242880 | tf_op jit(solution)/shard_map/all_gather | solution.py:99
  403.9 2.2 copy-start.1
  406.2 49.1 %copy-start.13 = (f32[1024]{0:T(1024)S(1)}, f32[1024]{0:T(1024)}, u32[]{:S(2)}) copy-start(f32[1024]{0:T(1024)} %param.22) | copy-start | bytes 12292
  408.3 172.1 %reduce-scatter.6.cloned.1.call-start = ((), (), s32[]{:S(2)}) async-start(), calls=%async_computation.7 | async-start | bytes 5242880 | tf_op jit(solution)/shard_map/reduce_scatter | solution.py:106
  483.8 0.7 copy-start.8
  483.8 96.6 %copy-start.2 = (bf16[512,1024]{1,0:T(8,128)(2,1)S(1)}, bf16[512,1024]{1,0:T(8,128)(2,1)}, u32[]{:S(2)}) copy-start(bf16[512,1024]{1,0:T(8,128)(2,1)} %add_convert_fusion.1) | copy-start | bytes 3145732
  483.8 112.0 %reduce-scatter.8.cloned.1.call-start = ((), (), s32[]{:S(2)}) async-start(), calls=%async_computation.8 | async-start | bytes 163840 | tf_op jit(solution)/shard_map/reduce_scatter | solution.py:118
  580.4 5.0 copy-start.14
  580.4 6.2 copy-start.9
  580.4 3.4 copy-start.4
Sparse Core Ops, SparseCore 0:
  9.0 48.3 all-gather.3
  60.5 83.7 all-gather.5
  328.1 75.7 reduce-scatter.3
  408.4 46.8 all-gather.7
  483.9 47.6 reduce-scatter.5
  585.3 10.4 reduce-scatter.7
where the time goes:
time: 1030 us; the launch traced here: 1020 us
  blocking collectives  369 us (36%)
  waiting for transfers between devices  258 us (25%)
  matrix products  177 us (17%)
  local copies, waits for them, and re-layouts  162 us (16%)
  other arithmetic  26.4 us (3%)
  between operations  14.5 us (1%)
  loops' own time  13.4 us (1%)
    unnamed x1, blocking collectives  176 us
    gather x3, local copies, waits for them, and re-layouts, shards(): jnp.take_along_axis(table, jnp.clip(local_rows, 0, held - 1), axis=1)  139 us
    all_gather x1, blocking collectives, shards(): lax.all_gather(embedding, 'dp', axis=0, tiled=True)  97.2 us
    all_gather x1, blocking collectives, shards(): lax.all_gather(candidates, 'dp', axis=0, tiled=True)  95.9 us
    all_gather x1, waiting for transfers between devices, shards(): every_prompt = lax.all_gather(prompts, 'dp', axis=0, tiled=True)  78.2 us
    reduce_scatter x1, waiting for transfers between devices, shards(): lax.psum_scatter(jnp.dot(context, w_out, preferred_element_type=jnp.float...  75.2 us
    dot_general x4, matrix products, attend(): jnp.einsum('hqk,khe->qhe', probs, all_values, preferred_element_type=jnp....  64.8 us
    sub x4, matrix products, attend(): weights = jnp.exp(logits - top)  57.9 us
  transfers between devices with their start and end apart: 6, of which 5 were waited for; matrix products, arithmetic and copies ran while one was open for 1% of the time, Pallas kernels for 0%

commit v1 on v0

--- a/solution.py
+++ b/solution.py
@@ -123,7 +123,9 @@
     embedding = (pooled * lax.rsqrt(square + 1e-06)).astype(jnp.bfloat16)
     asked_vectors, asked_rows = (
         lax.all_gather(embedding, "dp", axis=0, tiled=True),
-        lax.all_gather(candidates, "dp", axis=0, tiled=True),
+        jnp.concatenate(
+            lax.all_to_all(jnp.stack([candidates] * lax.axis_size("dp")), "dp", 0, 0), axis=0
+        ),
     )
     held = index_rows.shape[0]
     local_rows = asked_rows - lax.axis_index("dp") * held

time: 1030 us -> 986 us (0.957)
  blocking collectives: 369 us -> 273 us
  waiting for transfers between devices: 258 us -> 301 us
    all_gather x1 -> x0, blocking collectives: 95.9 us -> none  [shards(): lax.all_gather(candidates, 'dp', axis=0, tiled=True)]
    reduce_scatter x1, waiting for transfers between devices: 0.01 us -> 36.5 us  [shards(): lax.psum_scatter(jnp.dot(expanded, w_down, preferred_element_type=jnp.flo...]
  transfers between devices with their start and end apart: 6 -> 7, of which waited for: 5 -> 6; matrix products, arithmetic and copies ran while one was open for 1% -> 2% of each run, Pallas kernels for 0% -> 0%
where the time goes in v1:
time: 986 us; the launch traced here: 980 us
  waiting for transfers between devices  301 us (31%)
  blocking collectives  273 us (28%)
  matrix products  177 us (18%)
  local copies, waits for them, and re-layouts  163 us (17%)
  other arithmetic  27.2 us (3%)
  between operations  14.5 us (1%)
  loops' own time  13.4 us (1%)
    unnamed x1, blocking collectives  176 us
    gather x3, local copies, waits for them, and re-layouts, shards(): jnp.take_along_axis(table, jnp.clip(local_rows, 0, held - 1), axis=1)  139 us
    all_gather x1, blocking collectives, shards(): lax.all_gather(embedding, 'dp', axis=0, tiled=True)  97.2 us
    all_gather x1, waiting for transfers between devices, shards(): every_prompt = lax.all_gather(prompts, 'dp', axis=0, tiled=True)  78.2 us
    reduce_scatter x1, waiting for transfers between devices, shards(): lax.psum_scatter(jnp.dot(context, w_out, preferred_element_type=jnp.float...  75.2 us
    dot_general x4, matrix products, attend(): jnp.einsum('hqk,khe->qhe', probs, all_values, preferred_element_type=jnp....  64.8 us
    sub x4, matrix products, attend(): weights = jnp.exp(logits - top)  57.9 us
    all_gather x1, waiting for transfers between devices, shards(): whole = lax.all_gather(tokens, 'tensor', axis=0, tiled=True)  47.5 us
  transfers between devices with their start and end apart: 7, of which 6 were waited for; matrix products, arithmetic and copies ran while one was open for 2% of the time, Pallas kernels for 0%

profile of v1, /device:TPU:0, one launch (start us, length us, event | category | flops | bytes accessed | tf_op | source)
XLA Modules:
  0.0 979.9 jit_solution(8389069408068213677)
XLA Ops:
  9.9 47.5 %all-gather.4.cloned.1.call-done = bf16[2048,1024]{1,0:T(8,128)(2,1)} async-done(((bf16[512,1024]{1,0:T(8,128)(2,1)}), bf16[2048,1024]{1,0:T(8,128)(2,1)}) %all-gather.4.cloned.1.call-update) | async-done | bytes 4194320 | tf_op jit(solution)/shard_map/all_gather | solution.py:41
  57.4 3.7 convolution_convert_fusion.1
  61.5 2.3 convolution_convert_fusion.3
  63.7 2.3 fusion.48
  66.1 78.2 %all-gather.6.cloned.1.call-done = bf16[32,64,1024]{2,1,0:T(8,128)(2,1)} async-done(((bf16[1,64,1024]{2,1,0:T(8,128)(2,1)}), bf16[32,64,1024]{2,1,0:T(8,128)(2,1)}) %all-gather.6.cloned.1.call-update) | async-done | bytes 4194320 | tf_op jit(solution)/shard_map/all_gather | solution.py:47
  144.3 4.7 convolution_convert_fusion
  149.0 2.4 convolution_convert_fusion.2
  152.9 4.1 copy.29
  157.0 2.7 pad_maximum_fusion.1
  159.7 4.1 copy.30
  163.8 158.4 %while.11 = (s32[]{:T(128)}, bf16[4,512,256]{2,1,0:T(8,128)(2,1)}, s32[4]{0:T(128)S(1)}, s32[2048]{0:T(1024)S(1)}, s32[2048]{0:T(1024)S(1)}, /*index=5*/bf16[204...) while((s32[]{:T(128)}, bf16[4,512,256]{2,1,0:T(8,128)(2,1)}, ...), condition=%wide.region_6.7_spmd.clone, body=%wide.region_3.6_spmd.clone.sunk | while | flops 3284297728 | bytes 19714248 | solution.py:84
  169.6 14.5 %fusion.136 = f32[4,512]{1,0:T(4,128)S(1)} fusion(pred[512,4096]{1,0:T(8,128)(4,1)} %pad_add_fusion.2, bf16[512,4,64]{0,2,1:T(8,128)(2,1)S(1)} %bitcast.77, bf16[4096,4,64]{0,2,1:T(8,128)(2,1)} %get-tuple-element.208), kind=kOutput, calls=%fused_computation.130.clone.1 | convolution fusion | flops 1098911744 | bytes 4464640 | tf_op jit(solution)/shard_map/while/body/eval_jaxpr/sub | solution.py:78
  184.0 16.2 %fusion.137 = bf16[4,512,64]{1,2,0:T(8,128)(2,1)S(1)} fusion(bf16[4096,4,64]{0,2,1:T(8,128)(2,1)} %get-tuple-element.209, f32[4,512]{1,0:T(4,128)S(1)} %fusion.136, pred[512,4096]{1,0:T(8,128)(4,1)} %pad_add_fusion.2, bf16[512,4,64]{0,2,1:T(8,128)(2,1)S(1)} %bitcast.78, bf16[4096,4,64]{0,2,1:T(8,128)(2,1)} %get-tuple-element.208), kind=kOutput, calls=%fused_computation.14.clone.1 | convolution fusion | flops 2181175296 | bytes 6823936 | tf_op jit(solution)/shard_map/while/body/eval_jaxpr/hqk,khe->qhe/dot_general | solution.py:81
  206.5 14.5 %fusion.136 = f32[4,512]{1,0:T(4,128)S(1)} fusion(pred[512,4096]{1,0:T(8,128)(4,1)} %pad_add_fusion.2, bf16[512,4,64]{0,2,1:T(8,128)(2,1)S(1)} %bitcast.77, bf16[4096,4,64]{0,2,1:T(8,128)(2,1)} %get-tuple-element.208), kind=kOutput, calls=%fused_computation.130.clone.1 | convolution fusion | flops 1098911744 | bytes 4464640 | tf_op jit(solution)/shard_map/while/body/eval_jaxpr/sub | solution.py:78
  221.0 16.2 %fusion.137 = bf16[4,512,64]{1,2,0:T(8,128)(2,1)S(1)} fusion(bf16[4096,4,64]{0,2,1:T(8,128)(2,1)} %get-tuple-element.209, f32[4,512]{1,0:T(4,128)S(1)} %fusion.136, pred[512,4096]{1,0:T(8,128)(4,1)} %pad_add_fusion.2, bf16[512,4,64]{0,2,1:T(8,128)(2,1)S(1)} %bitcast.78, bf16[4096,4,64]{0,2,1:T(8,128)(2,1)} %get-tuple-element.208), kind=kOutput, calls=%fused_computation.14.clone.1 | convolution fusion | flops 2181175296 | bytes 6823936 | tf_op jit(solution)/shard_map/while/body/eval_jaxpr/hqk,khe->qhe/dot_general | solution.py:81
  243.5 14.5 %fusion.136 = f32[4,512]{1,0:T(4,128)S(1)} fusion(pred[512,4096]{1,0:T(8,128)(4,1)} %pad_add_fusion.2, bf16[512,4,64]{0,2,1:T(8,128)(2,1)S(1)} %bitcast.77, bf16[4096,4,64]{0,2,1:T(8,128)(2,1)} %get-tuple-element.208), kind=kOutput, calls=%fused_computation.130.clone.1 | convolution fusion | flops 1098911744 | bytes 4464640 | tf_op jit(solution)/shard_map/while/body/eval_jaxpr/sub | solution.py:78
  258.0 16.2 %fusion.137 = bf16[4,512,64]{1,2,0:T(8,128)(2,1)S(1)} fusion(bf16[4096,4,64]{0,2,1:T(8,128)(2,1)} %get-tuple-element.209, f32[4,512]{1,0:T(4,128)S(1)} %fusion.136, pred[512,4096]{1,0:T(8,128)(4,1)} %pad_add_fusion.2, bf16[512,4,64]{0,2,1:T(8,128)(2,1)S(1)} %bitcast.78, bf16[4096,4,64]{0,2,1:T(8,128)(2,1)} %get-tuple-element.208), kind=kOutput, calls=%fused_computation.14.clone.1 | convolution fusion | flops 2181175296 | bytes 6823936 | tf_op jit(solution)/shard_map/while/body/eval_jaxpr/hqk,khe->qhe/dot_general | solution.py:81
  280.5 14.5 %fusion.136 = f32[4,512]{1,0:T(4,128)S(1)} fusion(pred[512,4096]{1,0:T(8,128)(4,1)} %pad_add_fusion.2, bf16[512,4,64]{0,2,1:T(8,128)(2,1)S(1)} %bitcast.77, bf16[4096,4,64]{0,2,1:T(8,128)(2,1)} %get-tuple-element.208), kind=kOutput, calls=%fused_computation.130.clone.1 | convolution fusion | flops 1098911744 | bytes 4464640 | tf_op jit(solution)/shard_map/while/body/eval_jaxpr/sub | solution.py:78
  295.0 16.2 %fusion.137 = bf16[4,512,64]{1,2,0:T(8,128)(2,1)S(1)} fusion(bf16[4096,4,64]{0,2,1:T(8,128)(2,1)} %get-tuple-element.209, f32[4,512]{1,0:T(4,128)S(1)} %fusion.136, pred[512,4096]{1,0:T(8,128)(4,1)} %pad_add_fusion.2, bf16[512,4,64]{0,2,1:T(8,128)(2,1)S(1)} %bitcast.78, bf16[4096,4,64]{0,2,1:T(8,128)(2,1)} %get-tuple-element.208), kind=kOutput, calls=%fused_computation.14.clone.1 | convolution fusion | flops 2181175296 | bytes 6823936 | tf_op jit(solution)/shard_map/while/body/eval_jaxpr/hqk,khe->qhe/dot_general | solution.py:81
  322.2 5.8 fusion.100
  328.8 75.2 %reduce-scatter.4.cloned.1.call-done = f32[512,1024]{1,0:T(8,128)} async-done(((f32[2048,1024]{1,0:T(8,128)}), f32[512,1024]{1,0:T(8,128)}) %reduce-scatter.4.cloned.1.call-update) | async-done | bytes 2097168 | tf_op jit(solution)/shard_map/reduce_scatter | solution.py:88
  404.0 2.0 fusion.52
  408.4 46.9 %all-gather.8.cloned.1.call-done = bf16[2048,1024]{1,0:T(8,128)(2,1)} async-done(((bf16[512,1024]{1,0:T(8,128)(2,1)}), bf16[2048,1024]{1,0:T(8,128)(2,1)}) %all-gather.8.cloned.1.call-update) | async-done | bytes 4194320 | tf_op jit(solution)/shard_map/all_gather | solution.py:99
  455.3 28.5 %fusion.43 = bf16[2048,1024]{1,0:T(8,128)(2,1)} fusion(bf16[1024,1024]{1,0:T(8,128)(2,1)S(1)} %copy-done, f32[1024]{0:T(1024)S(1)} %copy-done.13, bf16[2048,1024]{1,0:T(8,128)(2,1)} %all-gather.8.cloned.1.call-done, bf16[1024,1024]{1,0:T(8,128)(2,1)} %param.21), kind=kOutput, calls=%fused_computation.47 | convolution fusion | flops 8730443776 | bytes 12587008 | tf_op jit(solution)/shard_map/dot_general | solution.py:107
  485.3 9.6 all-to-all-start
  495.0 36.5 %reduce-scatter.6.cloned.1.call-done = bf16[512,1024]{1,0:T(8,128)(2,1)} async-done(((bf16[2048,1024]{1,0:T(8,128)(2,1)}), bf16[512,1024]{1,0:T(8,128)(2,1)}) %reduce-scatter.6.cloned.1.call-update) | async-done | bytes 1048592 | tf_op jit(solution)/shard_map/reduce_scatter | solution.py:106
  533.2 1.7 multiply_reduce_fusion
  539.2 15.3 %reduce-scatter.8.cloned.1.call-done = f32[8,1024]{1,0:T(8,128)} async-done(((f32[32,1024]{1,0:T(8,128)}), f32[8,1024]{1,0:T(8,128)}) %reduce-scatter.8.cloned.1.call-update) | async-done | bytes 32784 | tf_op jit(solution)/shard_map/reduce_scatter | solution.py:118
  556.4 97.2 %all_gather.15 = bf16[256,1024]{1,0:T(8,128)(2,1)S(1)} all-gather(bf16[8,1024]{1,0:T(8,128)(2,1)S(1)} %multiply_convert_fusion), channel_id=1, replica_groups=mesh['dp'=32,'tensor'=4] {'dp'}, dimensions={0}, use_global_device_ids=true | all-gather | bytes 540672 | tf_op jit(solution)/shard_map/all_gather | solution.py:125
  653.5 3.5 convolution_multiply_fusion
  657.0 138.8 %gather_fusion = bf16[16384]{0:T(1024)(128)(2,1)S(1)} fusion(bf16[256,2048]{1,0:T(8,128)(2,1)S(1)} %convolution_multiply_fusion, s32[16384]{0:T(1024)S(1)} %reshape.150), kind=kCustom, calls=%fused_computation | custom fusion | bytes 196608 | tf_op jit(solution)/shard_map/jit(take_along_axis)/gather | solution.py:134
  796.1 176.2 %all-reduce = bf16[256,64]{1,0:T(8,128)(2,1)S(1)} all-reduce(bf16[256,64]{1,0:T(8,128)(2,1)S(1)} %select_convert_fusion), channel_id=5, replica_groups=mesh['dp'=32,'tensor'=4] {'dp'}, use_global_device_ids=true, to_apply=%region_15.16.clone | all-reduce | flops 16384 | bytes 65536
  (117 shorter events, 39.8 us)
Async XLA Ops:
  6.5 448.8 %copy-start = (bf16[1024,1024]{1,0:T(8,128)(2,1)S(1)}, bf16[1024,1024]{1,0:T(8,128)(2,1)}, u32[]{:S(2)}) copy-start(bf16[1024,1024]{1,0:T(8,128)(2,1)} %param.23) | copy-start | bytes 6291460
  6.5 50.9 %all-gather.4.cloned.1.call-start = ((), (), s32[]{:S(2)}) async-start(), calls=%async_computation.4 | async-start | bytes 5242880 | tf_op jit(solution)/shard_map/all_gather | solution.py:41
  7.3 137.0 %all-gather.6.cloned.1.call-start = ((), (), s32[]{:S(2)}) async-start(), calls=%async_computation.5 | async-start | bytes 4325376 | tf_op jit(solution)/shard_map/all_gather | solution.py:47
  8.0 396.0 %reduce-scatter.4.cloned.1.call-start = ((), (), s32[]{:S(2)}) async-start(), calls=%async_computation.6 | async-start | bytes 10485760 | tf_op jit(solution)/shard_map/reduce_scatter | solution.py:88
  57.4 3.7 copy-start.10
  57.4 4.1 copy-start.12
  144.3 4.7 copy-start.11
  149.0 2.4 copy-start.5
  328.0 0.7 copy-start.6
  328.0 0.7 copy-start.7
  328.1 75.9 %copy-start.3 = (bf16[512,1024]{1,0:T(8,128)(2,1)S(1)}, bf16[512,1024]{1,0:T(8,128)(2,1)}, u32[]{:S(2)}) copy-start(bf16[512,1024]{1,0:T(8,128)(2,1)} %param.15) | copy-start | bytes 3145732
  328.1 127.2 %all-gather.8.cloned.1.call-start = ((), (), s32[]{:S(2)}) async-start(), calls=%async_computation.7 | async-start | bytes 5242880 | tf_op jit(solution)/shard_map/all_gather | solution.py:99
  404.0 2.2 copy-start.1
  406.2 49.1 %copy-start.13 = (f32[1024]{0:T(1024)S(1)}, f32[1024]{0:T(1024)}, u32[]{:S(2)}) copy-start(f32[1024]{0:T(1024)} %param.22) | copy-start | bytes 12292
  408.3 123.2 %reduce-scatter.6.cloned.1.call-start = ((), (), s32[]{:S(2)}) async-start(), calls=%async_computation.8 | async-start | bytes 5242880 | tf_op jit(solution)/shard_map/reduce_scatter | solution.py:106
  483.8 0.7 copy-start.8
  483.8 47.7 %copy-start.2 = (bf16[512,1024]{1,0:T(8,128)(2,1)S(1)}, bf16[512,1024]{1,0:T(8,128)(2,1)}, u32[]{:S(2)}) copy-start(bf16[512,1024]{1,0:T(8,128)(2,1)} %add_convert_fusion.1) | copy-start | bytes 3145732
  484.5 51.8 %copy-start.9 = (s32[1,32]{1,0:T(1,128)S(1)}, s32[1,32]{1,0:T(1,128)}, u32[]{:S(2)}) copy-start(s32[1,32]{1,0:T(1,128)} %param.25) | copy-start | bytes 388
  484.5 51.9 %copy-start.14 = (u32[128]{0:T(128)S(1)}, u32[128]{0:T(128)}, u32[]{:S(2)}) copy-start(u32[128]{0:T(128)} %constant.173) | copy-start | bytes 1540
  485.3 52.3 %all-to-all-start = ((s32[32,1,512]{2,1,0:T(1,128)}), s32[32,1,512]{2,1,0:T(1,128)S(1)}, u32[]{:S(2)}, u32[]{:S(2)}) async-start(s32[32,1,512]{2,1,0:T(1,128)} %reshape.159), calls=%async_computation | async-start | bytes 131072 | tf_op jit(solution)/shard_map/all_to_all | solution.py:127
  494.9 59.7 %reduce-scatter.8.cloned.1.call-start = ((), (), s32[]{:S(2)}) async-start(), calls=%async_computation.9 | async-start | bytes 163840 | tf_op jit(solution)/shard_map/reduce_scatter | solution.py:118
  531.5 3.4 copy-start.4
Sparse Core Ops, SparseCore 0:
  9.0 48.3 all-gather.3
  60.5 83.7 all-gather.5
  328.2 75.7 reduce-scatter.3
  408.4 46.8 all-gather.7
  484.0 47.5 reduce-scatter.5
  536.4 18.0 reduce-scatter.7
